TPU v7x, 32 devices: a whole 2x2x4 slice. The times are simulated.
32 devices in a mesh: dp: 8 (over z, x), own: 4 (over y, core).
Axes of the slice: x: 2, y: 2, z: 4, core: 2. Of those that a mesh axis runs over, the one named last changes fastest.
Arguments:
- grads_fc: bfloat16 [8, 4, 8, 200, 1600], P('dp', 'own'), may hold values from -180 to 180
- grads_ln: bfloat16 [8, 4, 1600], P('dp'), may hold values from -48 to 48
- grads_emb: bfloat16 [8, 4, 8, 4, 1600], P('dp', 'own'), may hold values from -48 to 48
- weights_fc: bfloat16 [4, 8, 200, 1600], P('own'), may hold values from -0.15625 to 0.15625
- basis: float32 [1600, 256], replicated, may hold values from -0.15625 to 0.15625
- fc_m: float32 [4, 8, 200, 256], P('own', 'dp'), may hold values from -0.6 to 0.6
- fc_v: float32 [4, 8, 200, 256], P('own', 'dp'), may hold values from 0.001 to 0.1
- ln_params: float32 [4, 1600], replicated, may hold values from -3 to 3
- ln_m: float32 [4, 1600], replicated, may hold values from -0.6 to 0.6
- ln_v: float32 [4, 1600], replicated, may hold values from 0.001 to 0.1
- emb_weights: bfloat16 [4, 8, 4, 1600], P('own'), may hold values from -0.29882812 to 0.29882812
- emb_m: float32 [4, 8, 4, 1600], P('own', 'dp'), may hold values from -0.6 to 0.6
- emb_v: float32 [4, 8, 4, 1600], P('own', 'dp'), may hold values from 0.001 to 0.1
- step_count: int32 [1], replicated, may hold values from 1 to 63
Outputs:
- fc_m_next: float32 [4, 8, 200, 256], P('own', 'dp')
- fc_v_next: float32 [4, 8, 200, 256], P('own', 'dp')
- fc_direction: float32 [4, 8, 200, 256], P('own', 'dp')
- weights_next: bfloat16 [4, 8, 200, 1600], P('own')
- basis_next: float32 [1600, 256], replicated
- ln_next: float32 [4, 1600], replicated
- ln_m_next: float32 [4, 1600], replicated
- ln_v_next: float32 [4, 1600], replicated
- emb_next: bfloat16 [4, 8, 4, 1600], P('own')
- emb_m_next: float32 [4, 8, 4, 1600], P('own', 'dp')
- emb_v_next: float32 [4, 8, 4, 1600], P('own', 'dp')
All inputs are finite; a program needn't handle non-finite values.
Results may differ from a plain program's by a relative error of at most 0.009.
Values may be sent and summed in bfloat16 or wider, within the bound.
No kernel may reach another device: no remote copies, remote signals or barrier semaphores. Data moves between devices by JAX's collectives and lax.ppermute only.
A program may use at most 128 MiB of HBM per device.

v0:
```python
import math
import jax
import jax.numpy as jnp
from jax import lax
from jax.sharding import PartitionSpec as P

FF = 6400
RANK = 256
NS_STEPS = 5
beta_one = 0.9
beta_two = 0.999
adam_eps = 1e-08
learn_rate = 0.02
galore_scale = 0.25


def adam_update(moment_one, moment_two, gradient, correct_one, correct_two):
    moment_one_new = beta_one * moment_one + (1.0 - beta_one) * gradient
    moment_two_new = beta_two * moment_two + (1.0 - beta_two) * gradient * gradient
    direction = moment_one_new / correct_one / (jnp.sqrt(moment_two_new / correct_two) + adam_eps)
    return (moment_one_new, moment_two_new, direction)


def orthogonalize(subspace):
    highest = lax.Precision.HIGHEST
    iterate = subspace * lax.rsqrt(jnp.sum(subspace * subspace) + 1e-06)
    for sweep_index in range(NS_STEPS):
        gram_matrix = jnp.dot(iterate.T, iterate, precision=highest)
        iterate = 1.5 * iterate - 0.5 * jnp.dot(iterate, gram_matrix, precision=highest)
    return iterate


def shards(
    grads_fc,
    grads_ln,
    grads_emb,
    weights_fc,
    basis,
    fc_m,
    fc_v,
    ln_params,
    ln_m,
    ln_v,
    emb_weights,
    emb_m,
    emb_v,
    step_count,
):
    highest = lax.Precision.HIGHEST
    replicas = lax.axis_size("dp")
    owners = lax.axis_size("own")
    replica = lax.axis_index("dp")
    row_count = grads_fc.shape[3]
    width = grads_fc.shape[4]
    rank_cols = basis.shape[1]
    emb_count = grads_emb.shape[3]
    fc_part, emb_part = (
        lax.psum_scatter(
            grads_fc.astype(jnp.float32).astype(jnp.bfloat16), "dp", scatter_dimension=2, tiled=True
        ).astype(jnp.float32),
        lax.psum_scatter(
            grads_emb.astype(jnp.float32).astype(jnp.bfloat16),
            "dp",
            scatter_dimension=2,
            tiled=True,
        ).astype(jnp.float32),
    )
    ln_sum = lax.psum(grads_ln.astype(jnp.float32), "dp").reshape(4, width)
    fc_rows = fc_part.reshape(row_count, width)
    proj_rows = jnp.dot(fc_rows, basis, precision=highest)
    partial_value = jnp.dot(fc_rows.T, proj_rows, precision=highest)
    emb_rows = emb_part.reshape(1, 1, emb_count, width)
    proj_square = jnp.sum(proj_rows * proj_rows)
    emb_square = jnp.sum(emb_rows * emb_rows)
    subspace, proj_total, emb_total = lax.psum(
        (partial_value, proj_square, emb_square), ("dp", "own")
    )
    grad_norm = jnp.sqrt(proj_total + emb_total + jnp.sum(ln_sum * ln_sum) + 1e-06)
    clip_limit = math.sqrt(FF * RANK + emb_count * replicas * owners * width + 4 * width)
    factor = jnp.minimum(1.0, clip_limit / grad_norm)
    count = step_count[0].astype(jnp.float32)
    correct_one = 1.0 - jnp.power(jnp.float32(beta_one), count)
    correct_two = 1.0 - jnp.power(jnp.float32(beta_two), count)
    fc_grad = factor * proj_rows.reshape(1, 1, row_count, rank_cols)
    fc_m_next, fc_v_next, fc_direction = adam_update(fc_m, fc_v, fc_grad, correct_one, correct_two)
    ln_m_next, ln_v_next, ln_direction = adam_update(
        ln_m, ln_v, factor * ln_sum, correct_one, correct_two
    )
    ln_next = ln_params - learn_rate * ln_direction
    emb_m_next, emb_v_next, emb_direction = adam_update(
        emb_m, emb_v, factor * emb_rows, correct_one, correct_two
    )
    emb_mine = lax.dynamic_index_in_dim(emb_weights[0], replica, 0, keepdims=False)
    emb_new_rows = (
        emb_mine.astype(jnp.float32) - learn_rate * emb_direction.reshape(emb_count, width)
    ).astype(jnp.bfloat16)
    emb_new_rows = emb_new_rows.reshape(1, 1, emb_count, width)
    weights_mine = lax.dynamic_index_in_dim(weights_fc[0], replica, 0, keepdims=False)
    update_rows = jnp.dot(fc_direction.reshape(row_count, rank_cols), basis.T, precision=highest)
    new_rows = (weights_mine.astype(jnp.float32) - learn_rate * galore_scale * update_rows).astype(
        jnp.bfloat16
    )
    weights_next, emb_next = (
        lax.all_gather(new_rows.reshape(1, 1, row_count, width), "dp", axis=1, tiled=True),
        lax.all_gather(emb_new_rows, "dp", axis=1, tiled=True),
    )
    basis_next = orthogonalize(subspace)
    return (
        fc_m_next,
        fc_v_next,
        fc_direction,
        weights_next,
        basis_next,
        ln_next,
        ln_m_next,
        ln_v_next,
        emb_next,
        emb_m_next,
        emb_v_next,
    )


def solution(mesh):
    in_specs = (
        P("dp", "own", None, None, None),
        P("dp", None, None),
        P("dp", "own", None, None, None),
        P("own", None, None, None),
        P(),
        P("own", "dp", None, None),
        P("own", "dp", None, None),
        P(),
        P(),
        P(),
        P("own", None, None, None),
        P("own", "dp", None, None),
        P("own", "dp", None, None),
        P(),
    )
    out_specs = (
        P("own", "dp", None, None),
        P("own", "dp", None, None),
        P("own", "dp", None, None),
        P("own", None, None, None),
        P(),
        P(),
        P(),
        P(),
        P("own", None, None, None),
        P("own", "dp", None, None),
        P("own", "dp", None, None),
    )
    return jax.shard_map(shards, mesh=mesh, in_specs=in_specs, out_specs=out_specs, check_vma=False)
```

profile of v0, /device:TPU:0, one launch (start us, length us, event | category | flops | bytes accessed | tf_op | source)
XLA Modules:
  0.0 450.5 jit_solution(5772148660004264576)
XLA Ops:
  7.2 0.0 copy-start
  7.2 0.0 reduce-scatter.6.cloned.1.call-start
  7.2 0.7 reduce-scatter.6.cloned.1.call-update
  7.9 0.0 all-reduce.7.cloned.1.call-start
  8.0 0.7 all-reduce.7.cloned.1.call-update
  8.7 0.0 all-reduce.5.cloned.1.call-start
  8.7 129.6 %reduce-scatter.6.cloned.1.call-done = bf16[1,1,1,200,1600]{4,3,2,1,0:T(8,128)(2,1)} async-done(((bf16[1,1,8,200,1600]{4,3,2,1,0:T(8,128)(2,1)}), bf16[1,1,1,200,1600]{4,3,2,1,0:T(8,128)(2,1)}) %reduce-scatter.6.cloned.1.call-update) | async-done | bytes 640016
  138.4 0.0 copy-done
  138.4 0.0 copy-start.2
  138.4 2.7 multiply_reduce_fusion.1
  141.1 0.0 copy-done.2
  141.1 0.0 copy-start.12
  141.1 0.0 copy-start.11
  141.1 0.0 copy-start.4
  141.1 0.0 copy-start.5
  141.1 2.2 convolution_bitcast_fusion
  143.3 0.0 all-reduce.5.cloned.1.call-update
  143.3 0.0 all-gather.3.cloned.1.call-start
  144.1 0.0 copy-done.12
  144.1 0.6 dynamic-slice.2
  144.7 0.0 copy-done.11
  144.7 35.3 %psum.30 = f32[1,4,1600]{2,1,0:T(4,128)S(1)} all-reduce(bf16[1,4,1600]{2,1,0:T(4,128)(2,1)S(1)} %copy-done.11), channel_id=1, replica_groups=mesh['dp'=8,'own'=4] {'dp'}, use_global_device_ids=true, to_apply=%region_6.0 | all-reduce | flops 6400 | bytes 38400 | tf_op jit(solution)/shard_map/psum | solution.py:68
  179.9 0.6 multiply_reduce_fusion.2
  180.6 29.6 %all-reduce.7.cloned.1.call-done = bf16[1,1,8,4,1600]{4,3,2,1,0:T(4,128)(2,1)} async-done(((bf16[1,1,8,4,1600]{4,3,2,1,0:T(4,128)(2,1)}), bf16[1,1,8,4,1600]{4,3,2,1,0:T(4,128)(2,1)}) %all-reduce.7.cloned.1.call-update) | async-done | bytes 102416
  210.2 2.0 fusion.18
  213.4 40.6 %psum.32 = f32[]{:T(128)} all-reduce(f32[]{:T(128)S(6)} %add.66), channel_id=1, replica_groups=mesh['dp'=8,'own'=4] {'dp','own'}, use_global_device_ids=true, to_apply=%region_2.0 | all-reduce | flops 1 | bytes 8 | tf_op jit(solution)/shard_map/psum | solution.py:75
  255.4 0.0 copy-done.4
  255.4 0.0 copy-done.5
  255.4 0.9 multiply_divide_fusion
  256.3 0.0 copy-start.3
  256.3 0.0 copy-start.6
  256.3 0.0 copy-start.7
  256.3 0.0 copy-start.8
  256.3 0.0 copy-start.9
  256.3 0.0 copy-start.10
  256.3 3.8 fusion.6
  260.1 0.0 all-gather.3.cloned.1.call-update
  260.1 0.0 copy-done.3
  260.2 0.0 copy-done.6
  260.2 0.0 copy-done.7
  260.2 2.0 fusion.25
  262.2 30.7 %all_gather.7 = bf16[1,8,4,1600]{3,2,0,1:T(4,128)(2,1)S(1)} all-gather(bf16[1,1,4,1600]{3,2,0,1:T(4,128)(2,1)S(1)} %get-tuple-element.22), channel_id=1, replica_groups=mesh['dp'=8,'own'=4] {'dp'}, dimensions={1}, use_global_device_ids=true | all-gather | bytes 115200 | tf_op jit(solution)/shard_map/all_gather | solution.py:105
  292.9 0.0 copy-done.8
  292.9 0.0 copy-done.9
  292.9 0.0 copy-done.10
  292.9 0.7 multiply_subtract_fusion
  293.6 54.7 %all-reduce.5.cloned.1.call-done = f32[1600,256]{1,0:T(8,128)} async-done(((f32[1600,256]{1,0:T(8,128)}), f32[1600,256]{1,0:T(8,128)}) %all-reduce.5.cloned.1.call-update) | async-done | bytes 1638416 | tf_op jit(solution)/shard_map/psum | solution.py:75
  348.3 0.0 copy-start.1
  348.3 2.6 multiply_reduce_fusion
  351.5 0.0 copy-done.1
  351.5 2.9 fusion.7
  354.5 1.6 fusion.4
  356.0 3.0 fusion.31
  359.0 1.5 fusion.3
  360.5 3.2 fusion.32
  363.7 1.5 fusion.2
  365.2 3.0 fusion.33
  368.2 1.5 fusion.1
  369.7 3.0 fusion.34
  372.7 2.7 fusion
  375.4 62.7 %all-gather.3.cloned.1.call-done = bf16[1600,1600]{1,0:T(8,128)(2,1)} async-done(((bf16[200,1600]{1,0:T(8,128)(2,1)}), bf16[1600,1600]{1,0:T(8,128)(2,1)}) %all-gather.3.cloned.1.call-update) | async-done | bytes 5120016 | tf_op jit(solution)/shard_map/all_gather | solution.py:104
  438.1 5.3 %copy.37 = bf16[1,8,200,1600]{3,2,1,0:T(8,128)(2,1)} copy(bf16[1,8,200,1600]{3,2,1,0:T(8,128)(2,1)} %bitcast.73) | data formatting | bytes 10240000
  443.3 0.6 copy.38
Async XLA Ops:
  7.2 131.2 %copy-start = (f32[1600,256]{1,0:T(8,128)S(1)}, f32[1600,256]{1,0:T(8,128)}, u32[]{:S(2)}) copy-start(f32[1600,256]{1,0:T(8,128)} %param.18) | copy-start | bytes 4915204
  7.2 131.2 %reduce-scatter.6.cloned.1.call-start = ((), (), s32[]{:S(2)}) async-start(), calls=%async_computation.4 | async-start | bytes 5990400
  7.9 202.2 %all-reduce.7.cloned.1.call-start = ((), (), s32[]{:S(2)}) async-start(), calls=%async_computation.3 | async-start | bytes 212992
  8.7 339.6 %all-reduce.5.cloned.1.call-start = ((), (), s32[]{:S(2)}) async-start(), calls=%async_computation.1 | async-start | bytes 3276800 | tf_op jit(solution)/shard_map/psum | solution.py:75
  138.4 2.7 copy-start.2
  141.1 3.0 copy-start.12
  141.1 3.6 copy-start.11
  141.1 114.3 %copy-start.4 = (f32[1,1,200,256]{3,2,1,0:T(8,128)S(1)}, f32[1,1,200,256]{3,2,1,0:T(8,128)}, u32[]{:S(2)}) copy-start(f32[1,1,200,256]{3,2,1,0:T(8,128)} %param.20) | copy-start | bytes 614404
  141.1 114.4 %copy-start.5 = (f32[1,1,200,256]{3,2,1,0:T(8,128)S(1)}, f32[1,1,200,256]{3,2,1,0:T(8,128)}, u32[]{:S(2)}) copy-start(f32[1,1,200,256]{3,2,1,0:T(8,128)} %param.19) | copy-start | bytes 614404
  143.3 294.8 %all-gather.3.cloned.1.call-start = ((), (), s32[]{:S(2)}) async-start(), calls=%async_computation.2 | async-start | bytes 5990400 | tf_op jit(solution)/shard_map/all_gather | solution.py:104
  256.3 3.8 copy-start.3
  256.3 3.8 copy-start.6
  256.3 3.9 copy-start.7
  256.3 36.6 %copy-start.8 = (f32[4,1600]{1,0:T(4,128)S(1)}, f32[4,1600]{1,0:T(4,128)}, u32[]{:S(2)}) copy-start(f32[4,1600]{1,0:T(4,128)} %param.21) | copy-start | bytes 76804
  256.3 36.6 %copy-start.9 = (f32[4,1600]{1,0:T(4,128)S(1)}, f32[4,1600]{1,0:T(4,128)}, u32[]{:S(2)}) copy-start(f32[4,1600]{1,0:T(4,128)} %param.23) | copy-start | bytes 76804
  256.3 36.6 %copy-start.10 = (f32[4,1600]{1,0:T(4,128)S(1)}, f32[4,1600]{1,0:T(4,128)}, u32[]{:S(2)}) copy-start(f32[4,1600]{1,0:T(4,128)} %param.22) | copy-start | bytes 76804
  348.3 3.3 copy-start.1
Sparse Core Ops, SparseCore 0:
  11.5 126.8 reduce-scatter.5
  142.1 68.0 all-reduce.6
  216.1 132.0 all-reduce.4
  351.1 86.8 all-gather.2
where the time goes:
time: 451 us
  waiting for transfers between devices  278 us (62%)
  blocking collectives  107 us (24%)
  matrix products  32.4 us (7%)
  between operations  18 us (4%)
  other arithmetic  8.74 us (2%)
  local copies, waits for them, and re-layouts  6.57 us (1%)
    unnamed x6, waiting for transfers between devices  161 us
    all_gather x1, waiting for transfers between devices, shards(): lax.all_gather(new_rows.reshape(1, 1, row_count, width), 'dp', axis=1, ti...  62.7 us
    psum x1, waiting for transfers between devices, shards(): lax.psum((partial_value, proj_square, emb_square), ('dp', 'own'))  54.7 us
    psum x1, blocking collectives, shards(): lax.psum((partial_value, proj_square, emb_square), ('dp', 'own'))  40.6 us
    psum x1, blocking collectives, shards(): ln_sum = lax.psum(grads_ln.astype(jnp.float32), 'dp').reshape(4, width)  35.3 us
    all_gather x1, blocking collectives, shards(): lax.all_gather(emb_new_rows, 'dp', axis=1, tiled=True)  30.7 us
    dot_general x5, matrix products, orthogonalize(): gram_matrix = jnp.dot(iterate.T, iterate, precision=highest)  15 us
  transfers between devices with their start and end apart: 4, of which 4 were waited for; matrix products, arithmetic and copies ran while one was open for 9% of the time, Pallas kernels for 0%

commit v1 on v0

--- a/solution.py
+++ b/solution.py
@@ -12,6 +12,18 @@
 adam_eps = 1e-08
 learn_rate = 0.02
 galore_scale = 0.25
+
+
+def collect(x, axis, dim):
+    ways, here, step = (lax.axis_size(axis), lax.axis_index(axis), x.shape[dim])
+    line, have = (x, 1)
+    while have < ways:
+        line = jnp.concatenate(
+            [line, lax.ppermute(line, axis, [(d, (d - have) % ways) for d in range(ways)])],
+            axis=dim,
+        )
+        have = 2 * have
+    return jnp.roll(line, here * step, axis=dim)
 
 
 def adam_update(moment_one, moment_two, gradient, correct_one, correct_two):
@@ -101,7 +113,7 @@
         jnp.bfloat16
     )
     weights_next, emb_next = (
-        lax.all_gather(new_rows.reshape(1, 1, row_count, width), "dp", axis=1, tiled=True),
+        collect(new_rows.reshape(1, 1, row_count, width), "dp", 1),
         lax.all_gather(emb_new_rows, "dp", axis=1, tiled=True),
     )
     basis_next = orthogonalize(subspace)

time: 451 us -> 557 us (1.24)
  waiting for transfers between devices: 278 us -> 365 us
  blocking collectives: 107 us -> 115 us
  starting transfers between devices: 0.16 us -> 6.18 us
    ppermute x0 -> x3, waiting for transfers between devices: none -> 94.7 us  [collect(): lax.ppermute(line, axis, [(d, (d - have) % ways) for d in range(ways)])]
    all_gather x1 -> x0, waiting for transfers between devices: 62.7 us -> none  [shards(): lax.all_gather(new_rows.reshape(1, 1, row_count, width), 'dp', axis=1, ti...]
    psum x1, waiting for transfers between devices: 54.7 us -> 111 us  [shards(): lax.psum((partial_value, proj_square, emb_square), ('dp', 'own'))]
    ppermute x0 -> x3, starting transfers between devices: none -> 6.06 us  [collect(): lax.ppermute(line, axis, [(d, (d - have) % ways) for d in range(ways)])]
    unnamed x6 -> x5, waiting for transfers between devices: 161 us -> 160 us
  transfers between devices with their start and end apart: 4 -> 6, of which waited for: 4 -> 4; matrix products, arithmetic and copies ran while one was open for 9% -> 7% of each run, Pallas kernels for 0% -> 0%
where the time goes in v1:
time: 557 us
  waiting for transfers between devices  365 us (66%)
  blocking collectives  115 us (21%)
  matrix products  31.6 us (6%)
  between operations  18.2 us (3%)
  other arithmetic  11.7 us (2%)
  local copies, waits for them, and re-layouts  8.94 us (2%)
  starting transfers between devices  6.18 us (1%)
    unnamed x5, waiting for transfers between devices  160 us
    psum x1, waiting for transfers between devices, shards(): lax.psum((partial_value, proj_square, emb_square), ('dp', 'own'))  111 us
    ppermute x3, waiting for transfers between devices, collect(): lax.ppermute(line, axis, [(d, (d - have) % ways) for d in range(ways)])  94.7 us
    psum x1, blocking collectives, shards(): lax.psum((partial_value, proj_square, emb_square), ('dp', 'own'))  39.8 us
    psum x1, blocking collectives, shards(): ln_sum = lax.psum(grads_ln.astype(jnp.float32), 'dp').reshape(4, width)  38.9 us
    all_gather x1, blocking collectives, shards(): lax.all_gather(emb_new_rows, 'dp', axis=1, tiled=True)  36.3 us
    dot_general x5, matrix products, orthogonalize(): gram_matrix = jnp.dot(iterate.T, iterate, precision=highest)  14.6 us
  transfers between devices with their start and end apart: 6, of which 4 were waited for; matrix products, arithmetic and copies ran while one was open for 7% of the time, Pallas kernels for 0%

profile of v1, /device:TPU:0, one launch (start us, length us, event | category | flops | bytes accessed | tf_op | source)
XLA Modules:
  0.0 556.9 jit_solution(16147131951746376995)
XLA Ops:
  7.2 0.0 copy-start
  7.2 0.0 all-reduce.7.cloned.1.call-start
  7.2 0.7 all-reduce.7.cloned.1.call-update
  7.9 0.0 copy-start.16
  7.9 0.0 copy-start.15
  8.0 0.0 reduce-scatter.6.cloned.1.call-start
  8.0 0.7 reduce-scatter.6.cloned.1.call-update
  8.7 0.0 all-reduce.5.cloned.1.call-start
  9.6 0.6 dynamic-slice.2
  10.2 38.9 %psum.30 = f32[1,4,1600]{2,1,0:T(4,128)S(1)} all-reduce(bf16[1,4,1600]{2,1,0:T(4,128)(2,1)S(1)} %copy-done.15), channel_id=1, replica_groups=mesh['dp'=8,'own'=4] {'dp'}, use_global_device_ids=true, to_apply=%region_6.0 | all-reduce | flops 6400 | bytes 38400 | tf_op jit(solution)/shard_map/psum | solution.py:80
  49.1 0.6 multiply_reduce_fusion.2
  49.7 33.4 %all-reduce.7.cloned.1.call-done = bf16[1,1,8,4,1600]{4,3,2,1,0:T(4,128)(2,1)} async-done(((bf16[1,1,8,4,1600]{4,3,2,1,0:T(4,128)(2,1)}), bf16[1,1,8,4,1600]{4,3,2,1,0:T(4,128)(2,1)}) %all-reduce.7.cloned.1.call-update) | async-done | bytes 102416
  83.1 2.0 fusion.19
  85.1 125.3 %reduce-scatter.6.cloned.1.call-done = bf16[1,1,1,200,1600]{4,3,2,1,0:T(8,128)(2,1)} async-done(((bf16[1,1,8,200,1600]{4,3,2,1,0:T(8,128)(2,1)}), bf16[1,1,1,200,1600]{4,3,2,1,0:T(8,128)(2,1)}) %reduce-scatter.6.cloned.1.call-update) | async-done | bytes 640016
  210.3 0.0 copy-done
  210.3 2.6 multiply_reduce_fusion.1
  214.3 39.8 %psum.32 = f32[]{:T(128)} all-reduce(f32[]{:T(128)S(6)} %add.76), channel_id=1, replica_groups=mesh['dp'=8,'own'=4] {'dp','own'}, use_global_device_ids=true, to_apply=%region_2.0 | all-reduce | flops 1 | bytes 8 | tf_op jit(solution)/shard_map/psum | solution.py:87
  255.4 0.9 multiply_divide_fusion
  256.3 3.8 constant_dynamic-update-slice_fusion.7
  260.0 3.3 collective-permute-start
  263.4 0.0 copy-done.6
  263.4 2.2 convolution_bitcast_fusion
  265.5 0.0 all-reduce.5.cloned.1.call-update
  265.6 0.0 copy-start.12
  265.6 0.0 copy-start.13
  265.6 0.0 copy-start.14
  265.6 2.0 fusion.26
  267.7 36.3 %all_gather.3 = bf16[1,8,4,1600]{3,2,0,1:T(4,128)(2,1)S(1)} all-gather(bf16[1,1,4,1600]{3,2,0,1:T(4,128)(2,1)S(1)} %get-tuple-element.22), channel_id=1, replica_groups=mesh['dp'=8,'own'=4] {'dp'}, dimensions={1}, use_global_device_ids=true | all-gather | bytes 115200 | tf_op jit(solution)/shard_map/all_gather | solution.py:117
  303.9 0.0 collective-permute-done
  303.9 1.3 pad_maximum_fusion.1
  305.2 0.6 collective-permute-start.1
  305.8 0.7 multiply_subtract_fusion
  306.4 0.9 constant_dynamic-update-slice_fusion.6
  307.3 110.6 %all-reduce.5.cloned.1.call-done = f32[1600,256]{1,0:T(8,128)} async-done(((f32[1600,256]{1,0:T(8,128)}), f32[1600,256]{1,0:T(8,128)}) %all-reduce.5.cloned.1.call-update) | async-done | bytes 1638416 | tf_op jit(solution)/shard_map/psum | solution.py:87
  417.9 2.6 multiply_reduce_fusion
  421.2 2.9 fusion.8
  424.1 0.0 copy-start.3
  424.1 0.0 copy-start.5
  424.1 1.5 fusion.4
  425.6 0.0 collective-permute-done.1
  425.6 0.0 copy-done.3
  425.6 0.0 copy-done.5
  425.6 1.7 pad_maximum_fusion
  427.3 2.2 collective-permute-start.2
  429.5 2.9 fusion.32
  432.4 0.0 slice-start
  432.4 1.4 fusion.3
  433.8 3.1 fusion.33
  436.9 0.0 slice-start.1
  436.9 1.4 fusion.2
  438.4 2.9 fusion.34
  441.3 0.0 slice-start.2
  441.3 1.4 fusion.1
  442.7 2.9 fusion.35
  445.6 2.6 fusion
  448.2 1.5 constant_dynamic-update-slice_fusion.5
  449.8 94.7 %collective-permute-done.2 = bf16[1,4,200,1600]{3,2,1,0:T(8,128)(2,1)S(1)} collective-permute-done((bf16[1,4,200,1600]{3,2,1,0:T(8,128)(2,1)S(1)}, bf16[1,4,200,1600]{3,2,1,0:T(8,128)(2,1)S(1)}, u32[]{:S(2)}, u32[]{:S(2)}) %collective-permute-start.2) | collective-permute-done | bytes 2560032 | tf_op jit(solution)/shard_map/ppermute | solution.py:22
  544.4 0.4 constant_dynamic-update-slice_fusion.4
  544.8 0.1 constant_dynamic-update-slice_fusion.3
  544.9 0.1 constant_dynamic-update-slice_fusion.2
  545.0 1.5 constant_dynamic-update-slice_fusion.1
  546.5 0.4 constant_dynamic-update-slice_fusion
  546.9 2.8 constant_dynamic-slice_fusion
  549.7 0.6 copy.43
  (26 shorter events, 0.0 us)
Async XLA Ops:
  7.2 203.2 %copy-start = (f32[1600,256]{1,0:T(8,128)S(1)}, f32[1600,256]{1,0:T(8,128)}, u32[]{:S(2)}) copy-start(f32[1600,256]{1,0:T(8,128)} %param.18) | copy-start | bytes 4915204
  7.2 75.9 %all-reduce.7.cloned.1.call-start = ((), (), s32[]{:S(2)}) async-start(), calls=%async_computation.2 | async-start | bytes 212992
  7.9 1.7 copy-start.16
  7.9 2.3 copy-start.15
  8.0 202.4 %reduce-scatter.6.cloned.1.call-start = ((), (), s32[]{:S(2)}) async-start(), calls=%async_computation.3 | async-start | bytes 5990400
  8.7 246.7 %copy-start.8 = (f32[1,1,200,256]{3,2,1,0:T(8,128)S(1)}, f32[1,1,200,256]{3,2,1,0:T(8,128)}, u32[]{:S(2)}) copy-start(f32[1,1,200,256]{3,2,1,0:T(8,128)} %param.20) | copy-start | bytes 614404
  8.7 246.7 %copy-start.9 = (f32[1,1,200,256]{3,2,1,0:T(8,128)S(1)}, f32[1,1,200,256]{3,2,1,0:T(8,128)}, u32[]{:S(2)}) copy-start(f32[1,1,200,256]{3,2,1,0:T(8,128)} %param.19) | copy-start | bytes 614404
  8.7 409.2 %all-reduce.5.cloned.1.call-start = ((), (), s32[]{:S(2)}) async-start(), calls=%async_computation.1 | async-start | bytes 3276800 | tf_op jit(solution)/shard_map/psum | solution.py:87
  256.3 3.8 copy-start.7
  256.3 7.1 %copy-start.6 = (bf16[1,1,1,200,1600]{4,3,2,1,0:T(8,128)(2,1)S(1)}, bf16[1,1,1,200,1600]{4,3,2,1,0:T(8,128)(2,1)}, u32[]{:S(2)}) copy-start(bf16[1,1,1,200,1600]{4,3,2,1,0:T(8,128)(2,1)} %reduce-scatter.6.cloned.1.call-done) | copy-start | bytes 1920004
  260.0 43.9 %copy-start.2 = (bf16[1,1,200,1600]{3,2,1,0:T(8,128)(2,1)}, bf16[1,1,200,1600]{3,2,1,0:T(8,128)(2,1)S(1)}, u32[]{:S(2)}) copy-start(bf16[1,1,200,1600]{3,2,1,0:T(8,128)(2,1)S(1)} %get-tuple-element.34) | copy-start | bytes 1920004
  260.0 5.5 copy-start.10
  260.0 5.5 copy-start.11
  260.0 43.9 %collective-permute-start = (bf16[1,1,200,1600]{3,2,1,0:T(8,128)(2,1)S(1)}, bf16[1,1,200,1600]{3,2,1,0:T(8,128)(2,1)S(1)}, u32[]{:S(2)}, u32[]{:S(2)}) collective-permute-start(bf16[1,1,200,1600]{3,2,1,0:T(8,128)(2,1)S(1)} %get-tuple-element.34), channel_id=1, source_target_pairs={{0,28},{4,0},{8,4},{12,8},{16,12},{20,16},{24,20},{28,24},{1,29},{... | collective-permute-start | bytes 1920008 | tf_op jit(solution)/shard_map/ppermute | solution.py:22
  265.6 40.2 %copy-start.12 = (f32[4,1600]{1,0:T(4,128)S(1)}, f32[4,1600]{1,0:T(4,128)}, u32[]{:S(2)}) copy-start(f32[4,1600]{1,0:T(4,128)} %param.21) | copy-start | bytes 76804
  265.6 40.2 %copy-start.13 = (f32[4,1600]{1,0:T(4,128)S(1)}, f32[4,1600]{1,0:T(4,128)}, u32[]{:S(2)}) copy-start(f32[4,1600]{1,0:T(4,128)} %param.23) | copy-start | bytes 76804
  265.6 40.2 %copy-start.14 = (f32[4,1600]{1,0:T(4,128)S(1)}, f32[4,1600]{1,0:T(4,128)}, u32[]{:S(2)}) copy-start(f32[4,1600]{1,0:T(4,128)} %param.22) | copy-start | bytes 76804
  303.9 3.4 copy-start.4
  305.2 120.4 %collective-permute-start.1 = (bf16[1,2,200,1600]{3,2,1,0:T(8,128)(2,1)}, bf16[1,2,200,1600]{3,2,1,0:T(8,128)(2,1)}, u32[]{:S(2)}, u32[]{:S(2)}) collective-permute-start(bf16[1,2,200,1600]{3,2,1,0:T(8,128)(2,1)} %pad_maximum_fusion.1), channel_id=1, source_target_pairs={{0,24},{4,28},{8,0},{12,4},{16,8},{20,12},{24,16},{28,20},{1,25},{... | collective-permute-start | bytes 3840008 | tf_op jit(solution)/shard_map/ppermute | solution.py:22
  417.9 3.3 copy-start.1
  424.1 1.5 copy-start.3
  424.1 1.5 copy-start.5
  427.3 117.1 %collective-permute-start.2 = (bf16[1,4,200,1600]{3,2,1,0:T(8,128)(2,1)S(1)}, bf16[1,4,200,1600]{3,2,1,0:T(8,128)(2,1)S(1)}, u32[]{:S(2)}, u32[]{:S(2)}) collective-permute-start(bf16[1,4,200,1600]{3,2,1,0:T(8,128)(2,1)S(1)} %pad_maximum_fusion), channel_id=1, source_target_pairs={{0,16},{4,20},{8,24},{12,28},{16,0},{20,4},{24,8},{28,12},{1,17},{... | collective-permute-start | bytes 7680008 | tf_op jit(solution)/shard_map/ppermute | solution.py:22
  432.4 15.9 %slice-start = ((s8[10649600]{0:T(1024)(128)(4,1)}), s8[4194304]{0:T(1024)(128)(4,1)S(1)}, s32[]{:S(2)}) async-start(s8[10649600]{0:T(1024)(128)(4,1)} %bitcast.76), calls=%async_computation.4 | async-start | bytes 8388608
  436.9 11.3 %slice-start.1 = ((s8[10649600]{0:T(1024)(128)(4,1)}), s8[4194304]{0:T(1024)(128)(4,1)S(1)}, s32[]{:S(2)}) async-start(s8[10649600]{0:T(1024)(128)(4,1)} %bitcast.76), calls=%async_computation.5 | async-start | bytes 8388608
  441.3 7.0 %slice-start.2 = ((s8[10649600]{0:T(1024)(128)(4,1)}), s8[2260992]{0:T(1024)(128)(4,1)S(1)}, s32[]{:S(2)}) async-start(s8[10649600]{0:T(1024)(128)(4,1)} %bitcast.76), calls=%async_computation.6 | async-start | bytes 4521984
Sparse Core Ops, SparseCore 0:
  11.4 71.6 all-reduce.6
  87.0 123.3 reduce-scatter.5
  265.7 152.1 all-reduce.4
